TPU v7x, 256 devices: a whole 4x4x8 slice. The times are simulated.
256 devices in a mesh: dp: 16 (over z_lo, x), tensor: 16 (over y, z_hi, core).
Axes of the slice: x: 4, y: 4, z: 8 (z_hi: 2, z_lo: 4; z = z_hi * 4 + z_lo), core: 2. Of those that a mesh axis runs over, the one named last changes fastest.
Arguments:
- inner_x: bfloat16 [16, 2048, 7168], P('dp', None, 'tensor')
- gate_z: bfloat16 [16, 2048, 7168], P('dp', None, 'tensor'), may hold values from -6 to 6
- input_b: bfloat16 [16, 2048, 128], P('dp'), may hold values from -0.75 to 0.75
- output_c: bfloat16 [16, 2048, 128], P('dp'), may hold values from -6 to 6
- step_raw: float32 [16, 2048, 112], P('dp', None, 'tensor'), may hold values from -6 to 6
- decay_rate: float32 [112], P('tensor'), may hold values from 0.001 to 0.05
- skip_gain: float32 [112], P('tensor'), may hold values from 0.5 to 1.5
- norm_gain: float32 [7168], P('tensor'), may hold values from 0.5 to 1.5
- out_weight: bfloat16 [7168, 3584], P('tensor'), may hold values from -0.0625 to 0.0625
- segment: int32 [16, 2048], P('dp'), may hold values from 0 to 7, never falling along the last dimension, each value on 1 to 1024 neighbouring positions
- cache_slot: int32 [16, 8], replicated, may hold values from 0 to 127, as said below
Outputs:
- mixed: bfloat16 [16, 2048, 3584], P('dp', 'tensor')
- cache: float32 [128, 112, 4096], P('dp', 'tensor')
Inputs may be any that keep to these rules, and one draw needn't show every extreme that they name: `segment`: in each group's row the prompt numbers never fall and every prompt 0 to 7 is present. `cache_slot`: every slot is named exactly once; slot // 8 is the owning group, and no two prompts of one group have the same owning group.
All inputs are finite; a program needn't handle non-finite values.
Results may differ from a plain program's by a relative error of at most 0.018.
Values may be sent and summed in bfloat16 or wider, within the bound.
No kernel may reach another device: no remote copies, remote signals or barrier semaphores. Data moves between devices by JAX's collectives and lax.ppermute only.
A program may use at most 192 MiB of HBM per device.

v0:
```python
import jax
import jax.numpy as jnp
from jax import lax
from jax.sharding import Mesh, PartitionSpec as P

HEADS = 112
HEAD = 64
STATE = 64
NGROUPS = 2
REQS = 8
BLOCK = 256
INNER = 7168
HIGHEST = lax.Precision.HIGHEST
TENSOR = ("head_group", "y_rest", "z_hi", "core")
GROUP_MATES = TENSOR[1:]
NEAR_FIRST = ("head_group", "y_rest", "core")
FAR_LAST = "z_hi"


def split_pair(values):
    upper = values.astype(jnp.bfloat16)
    lower = (values - upper.astype(jnp.float32)).astype(jnp.bfloat16)
    return (upper, lower)


def split_einsum(form, wide, narrow):
    upper, lower = split_pair(wide)
    first = jnp.einsum(form, upper, narrow, preferred_element_type=jnp.float32)
    return first + jnp.einsum(form, lower, narrow, preferred_element_type=jnp.float32)


def local(
    inner_x,
    gate_z,
    input_b,
    output_c,
    step_raw,
    decay_rate,
    skip_gain,
    norm_gain,
    out_weight,
    segment,
    cache_slot,
):
    stream_len = inner_x.shape[1]
    dev_width = inner_x.shape[2]
    dev_heads = decay_rate.shape[0]
    tensor_idx = lax.axis_index(TENSOR)
    group_idx = tensor_idx * dev_heads // (HEADS // NGROUPS)
    b_cols = lax.dynamic_slice_in_dim(input_b[0], group_idx * STATE, STATE, 1)
    c_cols = lax.dynamic_slice_in_dim(output_c[0], group_idx * STATE, STATE, 1)
    step_size = jax.nn.softplus(step_raw[0])
    cum_log = jnp.cumsum(-decay_rate[None, :] * step_size, axis=0)
    seg_row = segment[0]
    block_count = stream_len // BLOCK
    x_blk = inner_x[0].reshape(block_count, BLOCK, dev_heads, HEAD)
    cum_blk = cum_log.reshape(block_count, BLOCK, dev_heads)
    step_blk = step_size.reshape(block_count, BLOCK, dev_heads)
    seg_blk = seg_row.reshape(block_count, BLOCK)
    b_blk = b_cols.reshape(block_count, BLOCK, STATE)
    c_blk = c_cols.reshape(block_count, BLOCK, STATE)
    positions = jnp.arange(BLOCK)
    scores = jnp.einsum("btn,bsn->bts", c_blk, b_blk, preferred_element_type=jnp.float32)
    causal_mask = (positions[None, None, :] <= positions[None, :, None]) & (
        seg_blk[:, :, None] == seg_blk[:, None, :]
    )
    cum_t = cum_blk.transpose(0, 2, 1)
    log_gap = cum_t[:, :, :, None] - cum_t[:, :, None, :]
    weights = (
        jnp.exp(jnp.where(causal_mask[:, None], log_gap, -jnp.inf))
        * step_blk.transpose(0, 2, 1)[:, :, None, :]
        * scores[:, None]
    )
    intra_part = split_einsum("bhts,bshp->bthp", weights, x_blk)
    last_seg = seg_blk[:, -1]
    last_cum = cum_blk[:, -1]
    pull_back = (
        jnp.exp(last_cum[:, None, :] - cum_blk)
        * step_blk
        * (seg_blk == last_seg[:, None]).astype(jnp.float32)[:, :, None]
    )
    added = split_einsum("bshp,bsn->bhpn", pull_back[:, :, :, None] * x_blk, b_blk)
    prev_cum = jnp.concatenate([jnp.zeros((1, dev_heads), jnp.float32), last_cum[:-1]], axis=0)
    prev_seg = jnp.concatenate([jnp.full((1,), -1, seg_row.dtype), last_seg[:-1]], axis=0)
    blocks = jnp.arange(block_count)
    earlier = blocks[None, :] < blocks[:, None]
    mix_ok = earlier & (last_seg[None, :] == prev_seg[:, None])
    mix_gap = prev_cum[:, None, :] - last_cum[None, :, :]
    mix = jnp.exp(jnp.where(mix_ok[:, :, None], mix_gap, -jnp.inf))
    carried = jnp.sum(mix[:, :, :, None, None] * added[None], axis=1)
    live_rows = (seg_blk == prev_seg[:, None]).astype(jnp.float32)
    carry_decay = jnp.exp(cum_blk - prev_cum[:, None, :]) * live_rows[:, :, None]
    carry_part = split_einsum("bhpn,btn->bthp", carried, c_blk) * carry_decay[:, :, :, None]
    outputs = intra_part + carry_part + skip_gain[None, None, :, None] * x_blk.astype(jnp.float32)
    mixer_y = outputs.reshape(stream_len, dev_width)
    members = (seg_row[None, :] == jnp.arange(REQS)[:, None]).astype(jnp.float32)
    end_index = (
        jnp.sum((seg_row[None, :] <= jnp.arange(REQS)[:, None]).astype(jnp.int32), axis=1) - 1
    )
    at_end = (jnp.arange(stream_len)[None, :] == end_index[:, None]).astype(jnp.float32)
    end_cum = jnp.dot(at_end, cum_log, precision=HIGHEST)
    seg_end_cum = jnp.dot(members.T, end_cum, precision=HIGHEST)
    pull_all = jnp.exp(seg_end_cum - cum_log) * step_size
    weighted = (inner_x[0].reshape(stream_len, dev_heads, HEAD) * pull_all[:, :, None]).reshape(
        stream_len, dev_width
    )
    masked_b = (
        (members.astype(jnp.bfloat16)[:, :, None] * b_cols[None])
        .transpose(1, 0, 2)
        .reshape(stream_len, REQS * STATE)
    )
    finals = split_einsum("tc,tk->ck", weighted, masked_b)
    finals = (
        finals.reshape(dev_heads, HEAD, REQS, STATE)
        .transpose(2, 0, 1, 3)
        .reshape(REQS, dev_heads * HEAD * STATE)
    )
    gated = mixer_y * jax.nn.silu(gate_z[0].astype(jnp.float32))
    sum_sq = jnp.sum(gated * gated, axis=1)
    group_stat = lax.all_gather(sum_sq, GROUP_MATES, tiled=True)
    mean_sq = jnp.sum(group_stat.reshape(-1, stream_len), axis=0) / (INNER // NGROUPS)
    rounded = (gated * lax.rsqrt(mean_sq + 1e-05)[:, None] * norm_gain[None, :]).astype(
        jnp.bfloat16
    )
    sizes = [lax.axis_size(name) for name in TENSOR]
    rows = stream_len // (sizes[0] * sizes[1] * sizes[2] * sizes[3])
    reordered = (
        rounded.reshape(sizes[0], sizes[1], sizes[2], sizes[3], rows, dev_width)
        .transpose(0, 1, 3, 2, 4, 5)
        .reshape(stream_len, dev_width)
    )
    partial = jnp.dot(reordered, out_weight, preferred_element_type=jnp.float32).astype(
        jnp.bfloat16
    )
    near = lax.psum_scatter(partial, NEAR_FIRST, scatter_dimension=0, tiled=True)
    mixed = near
    dp_idx = lax.axis_index("dp")
    dp_size = lax.axis_size("dp")
    own_slots = lax.dynamic_slice_in_dim(cache_slot, dp_idx, 1, 0)[0]
    dest_hot = ((own_slots // REQS)[:, None] == jnp.arange(dp_size)[None, :]).astype(jnp.float32)
    outbound = jnp.dot(dest_hot.T, finals, precision=HIGHEST).reshape(
        dp_size, dev_heads, HEAD * STATE
    )
    inbound = lax.all_to_all(
        outbound.astype(jnp.bfloat16), "dp", split_axis=0, concat_axis=0, tiled=True
    ).astype(outbound.dtype)
    near, inbound = lax.optimization_barrier((mixed, inbound))
    far_idx = lax.axis_index(FAR_LAST)
    half = near.shape[0] // 2
    keep = lax.dynamic_slice_in_dim(near, far_idx * half, half, 0)
    send = lax.dynamic_slice_in_dim(near, (1 - far_idx) * half, half, 0)
    got = lax.ppermute(send, FAR_LAST, perm=[(0, 1), (1, 0)])
    projected = (keep.astype(jnp.float32) + got.astype(jnp.float32)).astype(jnp.bfloat16)
    mixed = projected[None]
    wanted = dp_idx * REQS + jnp.arange(REQS)
    take_hot = jnp.any(cache_slot[:, :, None] == wanted[None, None, :], axis=1).astype(jnp.float32)
    cache = jnp.dot(
        take_hot.T, inbound.reshape(dp_size, dev_heads * HEAD * STATE), precision=HIGHEST
    )
    return (mixed, cache.reshape(REQS, dev_heads, HEAD * STATE))


def solution(mesh):
    dp_size, tensor_size = mesh.devices.shape
    groups = NGROUPS
    rest = tensor_size // (2 * 2 * groups)
    split = Mesh(mesh.devices.reshape(dp_size, groups, rest, 2, 2), ("dp",) + TENSOR)
    tp = TENSOR
    in_specs = (
        P("dp", None, tp),
        P("dp", None, tp),
        P("dp", None, None),
        P("dp", None, None),
        P("dp", None, tp),
        P(tp),
        P(tp),
        P(tp),
        P(tp, None),
        P("dp", None),
        P(),
    )
    out_specs = (P("dp", tp, None), P("dp", tp, None))
    return jax.shard_map(local, mesh=split, in_specs=in_specs, out_specs=out_specs, check_vma=False)
```

profile of v0, /device:TPU:32, one launch (start us, length us, event | category | flops | bytes accessed | tf_op | source)
XLA Modules:
  0.0 264.6 jit_solution(3308803690519148081)
XLA Ops:
  18.3 3.3 %copy.253 = bf16[56,8,8,256]{3,2,1,0:T(8,128)(2,1)} copy(bf16[56,8,8,256]{3,1,2,0:T(8,128)(2,1)} %bitcast.156) | data formatting | bytes 3670016
  22.7 2.6 constant_dynamic-slice_fusion.1
  31.2 6.7 %fusion.4 = f32[8,7,256,64]{2,3,1,0:T(8,128)} fusion(f32[8,256,256]{2,1,0:T(8,128)S(1)} %fusion.39, f32[8,7,256]{2,1,0:T(8,128)S(1)} %get-tuple-element.10, f32[8,7,256]{2,1,0:T(8,128)S(1)} %copy.193, pred[8,256,256]{2,1,0:T(8,128)(4,1)S(1)} %compare_and_fusion, bf16[8,256,7,64]{1,0,3,2:T(8,128)(2,1)S(1)} %bitcast.150), kind=kOutput, calls=%fused_computation.7 | convolution fusion | flops 488112128 | bytes 8241152 | tf_op jit(solution)/shard_map/bhts,bshp->bthp/dot_general | solution.py:28
  37.9 6.9 %fusion.1 = f32[8,7,256,64]{2,3,1,0:T(8,128)} fusion(f32[8,256,256]{2,1,0:T(8,128)S(1)} %fusion.39, f32[8,7,256]{2,1,0:T(8,128)S(1)} %get-tuple-element.10, f32[8,7,256]{2,1,0:T(8,128)S(1)} %copy.193, pred[8,256,256]{2,1,0:T(8,128)(4,1)S(1)} %compare_and_fusion, bf16[8,256,7,64]{1,0,3,2:T(8,128)(2,1)S(1)} %bitcast.151), kind=kOutput, calls=%fused_computation.5 | convolution fusion | flops 499122176 | bytes 8241152 | tf_op jit(solution)/shard_map/bhts,bshp->bthp/dot_general | solution.py:29
  47.0 5.7 %reshape.356 = f32[2,2,2,2,128,448]{4,3,2,1,0,5:T(2,128)} reshape(bf16[1,2048,448]{1,2,0:T(8,128)(2,1)} %param.12) | data formatting | bytes 5505024 | tf_op jit(solution)/shard_map/convert_element_type | solution.py:118
  52.8 3.9 %copy.254 = f32[56,8,8,256]{3,2,1,0:T(8,128)S(1)} copy(f32[56,8,8,256]{3,1,2,0:T(8,128)} %bitcast.148) | data formatting | bytes 7340032
  62.0 4.5 %multiply_reduce_fusion.1 = (f32[8,256]{1,0:T(8,128)S(1)}, f32[8,256,7,64]{1,3,2,0:T(8,128)}) fusion(f32[8,256,7,64]{1,0,3,2:T(8,128)S(1)} %bitcast.161, bf16[8,256,7,64]{1,0,3,2:T(8,128)(2,1)S(1)} %bitcast.154, f32[7]{0:T(128)S(1)} %copy-done.21, f32[8,256,7]{1,2,0:T(8,128)S(1)} %copy-done.14, f32[8,256,7,64]{1,3,2,0:T(8,128)S(1)} %fusion.37, ...), kind=kOutput, calls=%fused_computation.24 | convolution fusion | flops 131201024 | bytes 21430300 | tf_op jit(solution)/shard_map/bhpn,btn->bthp/dot_general | solution.py:29
  66.5 21.6 %all_gather.3 = f32[16384]{0:T(1024)} all-gather(f32[2048]{0:T(1024)S(1)} %bitcast.185), channel_id=1, replica_groups=mesh['dp'=16,'head_group'=2,'y_rest'=2,'z_hi'=2,'core'=2] {'y_rest','z_h..., dimensions={0}, use_global_device_ids=true | all-gather | bytes 73728 | tf_op jit(solution)/shard_map/all_gather | solution.py:120
  89.0 5.4 %reshape.350 = f32[2,2,2,2,128,448]{4,3,5,2,1,0:T(2,128)} reshape(f32[8,256,7,64]{1,3,2,0:T(8,128)} %get-tuple-element.14) | data formatting | bytes 7340032 | tf_op jit(solution)/shard_map/reshape | solution.py:95
  94.5 4.9 %fusion.27 = bf16[2,2,2,2,128,448]{4,5,2,3,1,0:T(8,128)(2,1)S(1)} fusion(f32[448]{0:T(512)S(1)} %copy-done.19, f32[2,2,2,2,128]{4,3,2,1,0:T(2,128)S(1)} %bitcast.186, f32[2,2,2,2,128,448]{4,3,2,1,0,5:T(2,128)} %reshape.356, f32[2,2,2,2,128,448]{4,3,5,2,1,0:T(2,128)} %reshape.350), kind=kLoop, calls=%fused_computation.38 | loop fusion | flops 7340032 | bytes 9185024 | tf_op jit(solution)/shard_map/transpose | solution.py:129
  99.3 3.1 %copy.222 = bf16[2,2,2,2,128,448]{4,3,2,1,0,5:T(2,128)(2,1)} copy(bf16[2,2,2,2,128,448]{4,5,2,3,1,0:T(8,128)(2,1)S(1)} %fusion.27) | data formatting | bytes 3670016 | tf_op jit(solution)/shard_map/transpose | solution.py:129
  102.5 5.3 %reshape.352 = bf16[2048,448]{0,1:T(8,128)(2,1)} reshape(bf16[2,2,2,2,128,448]{4,3,2,1,0,5:T(2,128)(2,1)} %copy.222) | data formatting | bytes 3670016 | tf_op jit(solution)/shard_map/reshape | solution.py:130
  107.7 12.6 %convolution_convert_fusion = bf16[2048,3584]{1,0:T(8,128)(2,1)} fusion(bf16[2048,448]{0,1:T(8,128)(2,1)} %reshape.352, bf16[448,3584]{1,0:T(8,128)(2,1)S(1)} %copy-done), kind=kOutput, calls=%fused_computation | convolution fusion | flops 6584008704 | bytes 19726336 | tf_op jit(solution)/shard_map/dot_general | solution.py:132
  126.6 2.6 reshape.353
  129.3 3.1 %copy.324 = f32[7,64,8,64]{3,1,0,2:T(8,128)} copy(f32[7,64,8,64]{3,2,1,0:T(8,128)} %reshape.353) | data formatting | bytes 1835008 | tf_op jit(solution)/shard_map/reshape | solution.py:114
  132.3 3.0 %reshape.354 = f32[8,28672]{1,0:T(8,128)} reshape(f32[8,7,64,64]{3,2,1,0:T(8,128)} %bitcast.155) | data formatting | bytes 1835008 | tf_op jit(solution)/shard_map/reshape | solution.py:116
  139.1 8.4 %all-to-all-start = ((bf16[16,7,4096]{2,1,0:T(8,128)(2,1)}), bf16[16,7,4096]{2,1,0:T(8,128)(2,1)}, u32[]{:S(2)}, u32[]{:S(2)}) async-start(bf16[16,7,4096]{2,1,0:T(8,128)(2,1)} %copy.224), calls=%async_computation.1 | async-start | bytes 2097152 | tf_op jit(solution)/shard_map/all_to_all | solution.py:144
  147.5 26.5 %all-to-all-done = bf16[16,7,4096]{2,1,0:T(8,128)(2,1)} async-done(((bf16[16,7,4096]{2,1,0:T(8,128)(2,1)}), bf16[16,7,4096]{2,1,0:T(8,128)(2,1)}, u32[]{:S(2)}, u32[]{:S(2)}) %all-to-all-start) | async-done | bytes 917536 | tf_op jit(solution)/shard_map/all_to_all | solution.py:144
  174.0 2.8 %convert_element_type.193 = f32[16,7,4096]{2,1,0:T(8,128)} convert(bf16[16,7,4096]{2,1,0:T(8,128)(2,1)} %all-to-all-done) | non-fusion elementwise | flops 458752 | bytes 2752512 | tf_op jit(solution)/shard_map/convert_element_type | solution.py:146
  176.8 30.8 %reduce-scatter.2.cloned.1.call-done = bf16[256,3584]{1,0:T(8,128)(2,1)} async-done(((bf16[2048,3584]{1,0:T(8,128)(2,1)}), bf16[256,3584]{1,0:T(8,128)(2,1)}) %reduce-scatter.2.cloned.1.call-update) | async-done | bytes 1835024 | tf_op jit(solution)/shard_map/reduce_scatter | solution.py:135
  209.7 4.8 %collective-permute-start = (bf16[128,3584]{1,0:T(8,128)(2,1)}, bf16[128,3584]{1,0:T(8,128)(2,1)}, u32[]{:S(2)}, u32[]{:S(2)}) collective-permute-start(bf16[128,3584]{1,0:T(8,128)(2,1)} %constant_dynamic-slice_fusion), channel_id=1, source_target_pairs={{0,2},{2,0},{1,3},{3,1},{4,6},{6,4},{5,7},{7,5},{8,10},{10,8},{9,1... | collective-permute-start | bytes 2752520 | tf_op jit(solution)/shard_map/ppermute | solution.py:152
  214.7 4.2 %fusion.20 = f32[8,7,4096]{2,0,1:T(8,128)} fusion(pred[16,8]{0,1:T(8,128)(4,1)S(1)} %compare_reduce_fusion, f32[2,8,7,4096]{3,2,1,0:T(8,128)} %bitcast.149), kind=kOutput, calls=%fused_computation.30 | convolution fusion | flops 44040192 | bytes 2752640 | tf_op jit(solution)/shard_map/dot_general | solution.py:157
  218.8 36.3 %collective-permute-done = bf16[128,3584]{1,0:T(8,128)(2,1)} collective-permute-done((bf16[128,3584]{1,0:T(8,128)(2,1)}, bf16[128,3584]{1,0:T(8,128)(2,1)}, u32[]{:S(2)}, u32[]{:S(2)}) %collective-permute-start) | collective-permute-done | bytes 917536 | tf_op jit(solution)/shard_map/ppermute | solution.py:152
  255.2 2.6 fusion.35
  (108 shorter events, 38.7 us)
Async XLA Ops:
  7.2 100.6 %copy-start = (bf16[448,3584]{1,0:T(8,128)(2,1)S(1)}, bf16[448,3584]{1,0:T(8,128)(2,1)}, u32[]{:S(2)}) copy-start(bf16[448,3584]{1,0:T(8,128)(2,1)} %param.19) | copy-start | bytes 9633796
  7.2 14.6 %copy-start.12 = (f32[1,2048,7]{1,0,2:T(1,128)S(1)}, f32[1,2048,7]{1,0,2:T(1,128)}, u32[]{:S(2)}) copy-start(f32[1,2048,7]{1,0,2:T(1,128)} %param.15) | copy-start | bytes 172036
  7.2 200.4 %reduce-scatter.2.cloned.1.call-start = ((), (), s32[]{:S(2)}) async-start(), calls=%async_computation.2 | async-start | bytes 16515072 | tf_op jit(solution)/shard_map/reduce_scatter | solution.py:135
  26.5 3.9 %copy-start.11 = (f32[2048,7]{0,1:T(8,128)S(1)}, f32[2048,7]{0,1:T(8,128)}, u32[]{:S(2)}) copy-start(f32[2048,7]{0,1:T(8,128)} %reduce.3) | copy-start | bytes 172036
  26.5 3.9 %copy-start.15 = (f32[8,256]{1,0:T(8,128)S(1)}, f32[8,256]{1,0:T(8,128)}, u32[]{:S(2)}) copy-start(f32[8,256]{1,0:T(8,128)} %get-tuple-element.11) | copy-start | bytes 24580
  26.5 3.9 %copy-start.16 = (f32[8,256]{1,0:T(8,128)S(1)}, f32[8,256]{1,0:T(8,128)}, u32[]{:S(2)}) copy-start(f32[8,256]{1,0:T(8,128)} %get-tuple-element.12) | copy-start | bytes 24580
  26.5 4.7 %copy-start.1 = (bf16[56,8,8,256]{3,2,1,0:T(8,128)(2,1)S(1)}, bf16[56,8,8,256]{3,2,1,0:T(8,128)(2,1)}, u32[]{:S(2)}) copy-start(bf16[56,8,8,256]{3,2,1,0:T(8,128)(2,1)} %copy.253) | copy-start | bytes 5505028
  26.6 2.3 copy-start.6
  37.9 6.9 %copy-start.4 = (bf16[1,2048,448]{1,2,0:T(8,128)(2,1)S(1)}, bf16[1,2048,448]{1,2,0:T(8,128)(2,1)}, u32[]{:S(2)}) copy-start(bf16[1,2048,448]{1,2,0:T(8,128)(2,1)} %param.12) | copy-start | bytes 5505028
  52.8 3.9 %copy-start.2 = (bf16[56,8,8,256]{3,2,1,0:T(8,128)(2,1)S(1)}, bf16[56,8,8,256]{3,2,1,0:T(8,128)(2,1)}, u32[]{:S(2)}) copy-start(bf16[56,8,8,256]{3,2,1,0:T(8,128)(2,1)} %copy.253) | copy-start | bytes 5505028
  52.8 3.9 %copy-start.7 = (bf16[8,8,8,256]{3,2,1,0:T(8,128)(2,1)S(1)}, bf16[8,8,8,256]{3,2,1,0:T(8,128)(2,1)}, u32[]{:S(2)}) copy-start(bf16[8,8,8,256]{3,2,1,0:T(8,128)(2,1)} %copy-done.6) | copy-start | bytes 786436
  52.8 3.9 %copy-start.10 = (f32[8,256,7]{1,2,0:T(8,128)S(1)}, f32[8,256,7]{1,2,0:T(8,128)}, u32[]{:S(2)}) copy-start(f32[8,256,7]{1,2,0:T(8,128)} %get-tuple-element.9) | copy-start | bytes 172036
  57.3 2.6 copy-start.5
  58.1 2.5 copy-start.23
  59.9 0.9 copy-start.14
  59.9 0.9 copy-start.21
  59.9 2.1 copy-start.22
  89.0 5.4 %copy-start.19 = (f32[448]{0:T(512)S(1)}, f32[448]{0:T(512)}, u32[]{:S(2)}) copy-start(f32[448]{0:T(512)} %param.18) | copy-start | bytes 5380
  120.3 0.8 copy-start.9
  120.3 2.3 copy-start.3
  129.3 6.1 %copy-start.20 = (s32[8]{0:T(128)S(1)}, s32[8]{0:T(128)}, u32[]{:S(2)}) copy-start(s32[8]{0:T(128)} %get-tuple-element.15) | copy-start | bytes 100
  139.1 75.5 %copy-start.17 = (s32[16,8]{0,1:T(8,128)S(1)}, s32[16,8]{0,1:T(8,128)}, u32[]{:S(2)}) copy-start(s32[16,8]{0,1:T(8,128)} %param.21) | copy-start | bytes 1540
  139.1 34.9 %all-to-all-start = ((bf16[16,7,4096]{2,1,0:T(8,128)(2,1)}), bf16[16,7,4096]{2,1,0:T(8,128)(2,1)}, u32[]{:S(2)}, u32[]{:S(2)}) async-start(bf16[16,7,4096]{2,1,0:T(8,128)(2,1)} %copy.224), calls=%async_computation.1 | async-start | bytes 2097152 | tf_op jit(solution)/shard_map/all_to_all | solution.py:144
  209.7 45.4 %collective-permute-start = (bf16[128,3584]{1,0:T(8,128)(2,1)}, bf16[128,3584]{1,0:T(8,128)(2,1)}, u32[]{:S(2)}, u32[]{:S(2)}) collective-permute-start(bf16[128,3584]{1,0:T(8,128)(2,1)} %constant_dynamic-slice_fusion), channel_id=1, source_target_pairs={{0,2},{2,0},{1,3},{3,1},{4,6},{6,4},{5,7},{7,5},{8,10},{10,8},{9,1... | collective-permute-start | bytes 2752520 | tf_op jit(solution)/shard_map/ppermute | solution.py:152
  (3 other events, 2.0 us)
Sparse Core Ops, SparseCore 0:
  120.5 87.0 reduce-scatter.1
where the time goes:
time: 266 us; the launch traced here: 265 us
  waiting for transfers between devices  93.6 us (35%)
  local copies, waits for them, and re-layouts  50.7 us (19%)
  matrix products  45 us (17%)
  other arithmetic  26 us (10%)
  blocking collectives  21.6 us (8%)
  between operations  14.4 us (5%)
  starting transfers between devices  13.3 us (5%)
    ppermute x1, waiting for transfers between devices, local(): got = lax.ppermute(send, FAR_LAST, perm=[(0, 1), (1, 0)])  36.3 us
    reduce_scatter x1, waiting for transfers between devices, local(): lax.psum_scatter(partial, NEAR_FIRST, scatter_dimension=0, tiled=True)  30.8 us
    all_to_all x1, waiting for transfers between devices, local(): lax.all_to_all(outbound.astype(jnp.bfloat16), 'dp', split_axis=0, concat_...  26.5 us
    all_gather x1, blocking collectives, local(): group_stat = lax.all_gather(sum_sq, GROUP_MATES, tiled=True)  21.6 us
    dot_general x4, matrix products, split_einsum(): jnp.einsum(form, lower, narrow, preferred_element_type=jnp.float32)  14.1 us
    unnamed x62, local copies, waits for them, and re-layouts  13 us
    dot_general x1, matrix products, local(): jnp.dot(reordered, out_weight, preferred_element_type=jnp.float32)  12.6 us
    dot_general x4, matrix products, split_einsum(): first = jnp.einsum(form, upper, narrow, preferred_element_type=jnp.float32)  9.09 us
  transfers between devices with their start and end apart: 3, of which 3 were waited for; matrix products, arithmetic and copies ran while one was open for 9% of the time, Pallas kernels for 0%

commit v1 on v0

--- a/solution.py
+++ b/solution.py
@@ -117,7 +117,15 @@
     )
     gated = mixer_y * jax.nn.silu(gate_z[0].astype(jnp.float32))
     sum_sq = jnp.sum(gated * gated, axis=1)
-    group_stat = lax.all_gather(sum_sq, GROUP_MATES, tiled=True)
+    group_stat = jnp.concatenate(
+        lax.all_to_all(
+            jnp.stack(lax.axis_size(GROUP_MATES) * [sum_sq], 0),
+            split_axis=0,
+            axis_name=GROUP_MATES,
+            concat_axis=0,
+        ),
+        axis=0,
+    )
     mean_sq = jnp.sum(group_stat.reshape(-1, stream_len), axis=0) / (INNER // NGROUPS)
     rounded = (gated * lax.rsqrt(mean_sq + 1e-05)[:, None] * norm_gain[None, :]).astype(
         jnp.bfloat16

time: 266 us -> 244 us (0.917)
  blocking collectives: 21.6 us -> 0 us
  starting transfers between devices: 13.3 us -> 20.3 us
  local copies, waits for them, and re-layouts: 50.7 us -> 47.1 us
    all_gather x1 -> x0, blocking collectives: 21.6 us -> none  [local(): group_stat = lax.all_gather(sum_sq, GROUP_MATES, tiled=True)]
    all_to_all x0 -> x1, starting transfers between devices: none -> 8.57 us  [local(): lax.all_to_all(jnp.stack(lax.axis_size(GROUP_MATES) * [sum_sq], 0), split...]
    unnamed x62 -> x48, local copies, waits for them, and re-layouts: 13 us -> 9.3 us
  transfers between devices with their start and end apart: 3 -> 4, of which waited for: 3 -> 3; matrix products, arithmetic and copies ran while one was open for 9% -> 15% of each run, Pallas kernels for 0% -> 0%
where the time goes in v1:
time: 244 us; the launch traced here: 243 us
  waiting for transfers between devices  94.7 us (39%)
  local copies, waits for them, and re-layouts  47.1 us (19%)
  matrix products  42.9 us (18%)
  other arithmetic  23.7 us (10%)
  starting transfers between devices  20.3 us (8%)
  between operations  14.4 us (6%)
    ppermute x1, waiting for transfers between devices, local(): got = lax.ppermute(send, FAR_LAST, perm=[(0, 1), (1, 0)])  36.3 us
    reduce_scatter x1, waiting for transfers between devices, local(): lax.psum_scatter(partial, NEAR_FIRST, scatter_dimension=0, tiled=True)  32.1 us
    all_to_all x1, waiting for transfers between devices, local(): lax.all_to_all(outbound.astype(jnp.bfloat16), 'dp', split_axis=0, concat_...  26.3 us
    dot_general x4, matrix products, split_einsum(): jnp.einsum(form, lower, narrow, preferred_element_type=jnp.float32)  13.2 us
    dot_general x1, matrix products, local(): jnp.dot(reordered, out_weight, preferred_element_type=jnp.float32)  12.6 us
    unnamed x48, local copies, waits for them, and re-layouts  9.3 us
    all_to_all x1, starting transfers between devices, local(): lax.all_to_all(jnp.stack(lax.axis_size(GROUP_MATES) * [sum_sq], 0), split...  8.57 us
    dot_general x4, matrix products, split_einsum(): first = jnp.einsum(form, upper, narrow, preferred_element_type=jnp.float32)  8 us
  transfers between devices with their start and end apart: 4, of which 3 were waited for; matrix products, arithmetic and copies ran while one was open for 15% of the time, Pallas kernels for 0%

profile of v1, /device:TPU:32, one launch (start us, length us, event | category | flops | bytes accessed | tf_op | source)
XLA Modules:
  0.0 243.1 jit_solution(11160454687678256908)
XLA Ops:
  18.3 3.3 %copy.290 = bf16[56,8,8,256]{3,2,1,0:T(8,128)(2,1)} copy(bf16[56,8,8,256]{3,1,2,0:T(8,128)(2,1)} %bitcast.156) | data formatting | bytes 3670016
  22.7 2.6 %constant_dynamic-slice_fusion.1 = (bf16[1,2048,64]{2,1,0:T(8,128)(2,1)}, bf16[1,2048,64]{2,1,0:T(8,128)(2,1)}) fusion(bf16[1,2048,128]{2,1,0:T(8,128)(2,1)} %param.13, s32[]{:T(128)S(6)} %select_n.54, bf16[1,2048,128]{2,1,0:T(8,128)(2,1)} %param.14), kind=kLoop, calls=%fused_computation.95 | loop fusion | bytes 1048580 | tf_op jit(solution)/shard_map/dynamic_slice | solution.py:50
  30.5 5.6 %fusion.4 = f32[8,7,256,64]{2,3,1,0:T(8,128)S(1)} fusion(f32[8,256,256]{2,1,0:T(8,128)S(1)} %fusion.39, f32[8,7,256]{2,1,0:T(8,128)S(1)} %get-tuple-element.10, f32[8,7,256]{2,1,0:T(8,128)S(1)} %copy.228, pred[8,256,256]{2,1,0:T(8,128)(4,1)S(1)} %compare_and_fusion, bf16[8,256,7,64]{1,0,3,2:T(8,128)(2,1)S(1)} %bitcast.150), kind=kOutput, calls=%fused_computation.7 | convolution fusion | flops 488112128 | bytes 8241152 | tf_op jit(solution)/shard_map/bhts,bshp->bthp/dot_general | solution.py:28
  36.0 6.0 %fusion.1 = f32[8,7,256,64]{2,3,1,0:T(8,128)S(1)} fusion(f32[8,256,256]{2,1,0:T(8,128)S(1)} %fusion.39, f32[8,7,256]{2,1,0:T(8,128)S(1)} %get-tuple-element.10, f32[8,7,256]{2,1,0:T(8,128)S(1)} %copy.228, pred[8,256,256]{2,1,0:T(8,128)(4,1)S(1)} %compare_and_fusion, bf16[8,256,7,64]{1,0,3,2:T(8,128)(2,1)S(1)} %bitcast.151), kind=kOutput, calls=%fused_computation.5 | convolution fusion | flops 499122176 | bytes 8241152 | tf_op jit(solution)/shard_map/bhts,bshp->bthp/dot_general | solution.py:29
  48.1 4.5 %multiply_reduce_fusion.1 = (f32[8,256]{1,0:T(8,128)S(1)}, f32[8,256,7,64]{1,3,2,0:T(8,128)}) fusion(f32[8,256,7,64]{1,0,3,2:T(8,128)S(1)} %bitcast.161, bf16[8,256,7,64]{1,0,3,2:T(8,128)(2,1)S(1)} %bitcast.154, f32[7]{0:T(128)S(1)} %copy-done.16, f32[8,256,7]{1,2,0:T(8,128)S(1)} %get-tuple-element.8, f32[8,256,7,64]{1,3,2,0:T(8,128)S(1)} %fusion.37, ...), kind=kOutput, calls=%fused_computation.24 | convolution fusion | flops 131201024 | bytes 21430300 | tf_op jit(solution)/shard_map/bhpn,btn->bthp/dot_general | solution.py:29
  53.2 8.6 %all-to-all-start = ((f32[8,1,2048]{2,1,0:T(1,128)}), f32[8,1,2048]{2,1,0:T(1,128)S(1)}, u32[]{:S(2)}, u32[]{:S(2)}) async-start(f32[8,1,2048]{2,1,0:T(1,128)} %stack.5), calls=%async_computation | async-start | bytes 131072 | tf_op jit(solution)/shard_map/all_to_all | solution.py:121
  62.0 5.8 %reshape.362 = f32[2,2,2,2,128,448]{4,3,2,1,0,5:T(2,128)} reshape(bf16[1,2048,448]{1,2,0:T(8,128)(2,1)} %param.12) | data formatting | bytes 5505024 | tf_op jit(solution)/shard_map/convert_element_type | solution.py:118
  67.8 5.4 %reshape.357 = f32[2,2,2,2,128,448]{4,3,5,2,1,0:T(2,128)} reshape(f32[8,256,7,64]{1,3,2,0:T(8,128)} %get-tuple-element.14) | data formatting | bytes 7340032 | tf_op jit(solution)/shard_map/reshape | solution.py:95
  73.3 4.9 %fusion.27 = bf16[2,2,2,2,128,448]{4,5,2,3,1,0:T(8,128)(2,1)S(1)} fusion(f32[448]{0:T(512)S(1)} %copy-done.14, f32[2,2,2,2,128]{4,3,2,1,0:T(2,128)S(1)} %bitcast.186, f32[2,2,2,2,128,448]{4,3,2,1,0,5:T(2,128)} %reshape.362, f32[2,2,2,2,128,448]{4,3,5,2,1,0:T(2,128)} %reshape.357), kind=kLoop, calls=%fused_computation.38 | loop fusion | flops 7340032 | bytes 9185024 | tf_op jit(solution)/shard_map/transpose | solution.py:137
  78.2 3.1 %copy.258 = bf16[2,2,2,2,128,448]{4,3,2,1,0,5:T(2,128)(2,1)} copy(bf16[2,2,2,2,128,448]{4,5,2,3,1,0:T(8,128)(2,1)S(1)} %fusion.27) | data formatting | bytes 3670016 | tf_op jit(solution)/shard_map/transpose | solution.py:137
  81.3 5.3 %reshape.358 = bf16[2048,448]{0,1:T(8,128)(2,1)} reshape(bf16[2,2,2,2,128,448]{4,3,2,1,0,5:T(2,128)(2,1)} %copy.258) | data formatting | bytes 3670016 | tf_op jit(solution)/shard_map/reshape | solution.py:138
  86.6 12.6 %convolution_convert_fusion = bf16[2048,3584]{1,0:T(8,128)(2,1)} fusion(bf16[2048,448]{0,1:T(8,128)(2,1)} %reshape.358, bf16[448,3584]{1,0:T(8,128)(2,1)S(1)} %copy-done), kind=kOutput, calls=%fused_computation | convolution fusion | flops 6584008704 | bytes 19726336 | tf_op jit(solution)/shard_map/dot_general | solution.py:140
  105.5 2.6 %reshape.359 = f32[7,64,8,64]{3,2,1,0:T(8,128)} reshape(f32[448,512]{1,0:T(8,128)} %convolution_add_fusion) | data formatting | bytes 1835008 | tf_op jit(solution)/shard_map/reshape | solution.py:114
  108.1 3.1 %copy.361 = f32[7,64,8,64]{3,1,0,2:T(8,128)} copy(f32[7,64,8,64]{3,2,1,0:T(8,128)} %reshape.359) | data formatting | bytes 1835008 | tf_op jit(solution)/shard_map/reshape | solution.py:114
  111.2 3.3 %reshape.360 = f32[8,28672]{1,0:T(8,128)} reshape(f32[8,7,64,64]{3,2,1,0:T(8,128)} %bitcast.155) | data formatting | bytes 1835008 | tf_op jit(solution)/shard_map/reshape | solution.py:116
  114.5 2.2 convolution_convert_fusion.1
  118.2 6.6 %all-to-all-start.1 = ((bf16[16,7,4096]{2,1,0:T(8,128)(2,1)}), bf16[16,7,4096]{2,1,0:T(8,128)(2,1)}, u32[]{:S(2)}, u32[]{:S(2)}) async-start(bf16[16,7,4096]{2,1,0:T(8,128)(2,1)} %copy.260), calls=%async_computation.2 | async-start | bytes 2097152 | tf_op jit(solution)/shard_map/all_to_all | solution.py:152
  124.8 26.3 %all-to-all-done.1 = bf16[16,7,4096]{2,1,0:T(8,128)(2,1)} async-done(((bf16[16,7,4096]{2,1,0:T(8,128)(2,1)}), bf16[16,7,4096]{2,1,0:T(8,128)(2,1)}, u32[]{:S(2)}, u32[]{:S(2)}) %all-to-all-start.1) | async-done | bytes 917536 | tf_op jit(solution)/shard_map/all_to_all | solution.py:152
  151.1 2.8 %convert_element_type.193 = f32[16,7,4096]{2,1,0:T(8,128)} convert(bf16[16,7,4096]{2,1,0:T(8,128)(2,1)} %all-to-all-done.1) | non-fusion elementwise | flops 458752 | bytes 2752512 | tf_op jit(solution)/shard_map/convert_element_type | solution.py:154
  153.9 32.1 %reduce-scatter.2.cloned.1.call-done = bf16[256,3584]{1,0:T(8,128)(2,1)} async-done(((bf16[2048,3584]{1,0:T(8,128)(2,1)}), bf16[256,3584]{1,0:T(8,128)(2,1)}) %reduce-scatter.2.cloned.1.call-update) | async-done | bytes 1835024 | tf_op jit(solution)/shard_map/reduce_scatter | solution.py:143
  188.2 4.8 %collective-permute-start = (bf16[128,3584]{1,0:T(8,128)(2,1)}, bf16[128,3584]{1,0:T(8,128)(2,1)}, u32[]{:S(2)}, u32[]{:S(2)}) collective-permute-start(bf16[128,3584]{1,0:T(8,128)(2,1)} %constant_dynamic-slice_fusion), channel_id=1, source_target_pairs={{0,2},{2,0},{1,3},{3,1},{4,6},{6,4},{5,7},{7,5},{8,10},{10,8},{9,1... | collective-permute-start | bytes 2752520 | tf_op jit(solution)/shard_map/ppermute | solution.py:160
  193.1 4.2 %fusion.20 = f32[8,7,4096]{2,0,1:T(8,128)} fusion(pred[16,8]{0,1:T(8,128)(4,1)S(1)} %compare_reduce_fusion, f32[2,8,7,4096]{3,2,1,0:T(8,128)} %bitcast.149), kind=kOutput, calls=%fused_computation.30 | convolution fusion | flops 44040192 | bytes 2752640 | tf_op jit(solution)/shard_map/dot_general | solution.py:165
  197.3 36.3 %collective-permute-done = bf16[128,3584]{1,0:T(8,128)(2,1)} collective-permute-done((bf16[128,3584]{1,0:T(8,128)(2,1)}, bf16[128,3584]{1,0:T(8,128)(2,1)}, u32[]{:S(2)}, u32[]{:S(2)}) %collective-permute-start) | collective-permute-done | bytes 917536 | tf_op jit(solution)/shard_map/ppermute | solution.py:160
  233.6 2.6 %fusion.35 = bf16[1,128,3584]{2,1,0:T(8,128)(2,1)} fusion(bf16[128,3584]{1,0:T(8,128)(2,1)} %collective-permute-done, bf16[256,3584]{1,0:T(8,128)(2,1)} %reduce-scatter.2.cloned.1.call-done, s32[]{:T(128)S(6)} %select_n.58), kind=kLoop, calls=%fused_computation.46 | loop fusion | flops 1835008 | bytes 2752516 | tf_op jit(solution)/shard_map/broadcast_in_dim | solution.py:162
  (95 shorter events, 34.1 us)
Async XLA Ops:
  7.2 79.4 %copy-start = (bf16[448,3584]{1,0:T(8,128)(2,1)S(1)}, bf16[448,3584]{1,0:T(8,128)(2,1)}, u32[]{:S(2)}) copy-start(bf16[448,3584]{1,0:T(8,128)(2,1)} %param.19) | copy-start | bytes 9633796
  7.2 14.6 %copy-start.8 = (f32[1,2048,7]{1,0,2:T(1,128)S(1)}, f32[1,2048,7]{1,0,2:T(1,128)}, u32[]{:S(2)}) copy-start(f32[1,2048,7]{1,0,2:T(1,128)} %param.15) | copy-start | bytes 172036
  13.3 0.6 copy-start.5
  26.5 3.8 %copy-start.7 = (f32[2048,7]{0,1:T(8,128)S(1)}, f32[2048,7]{0,1:T(8,128)}, u32[]{:S(2)}) copy-start(f32[2048,7]{0,1:T(8,128)} %reduce.4) | copy-start | bytes 172036
  26.5 3.8 %copy-start.10 = (f32[8,256]{1,0:T(8,128)S(1)}, f32[8,256]{1,0:T(8,128)}, u32[]{:S(2)}) copy-start(f32[8,256]{1,0:T(8,128)} %get-tuple-element.11) | copy-start | bytes 24580
  26.5 3.8 %copy-start.11 = (f32[8,256]{1,0:T(8,128)S(1)}, f32[8,256]{1,0:T(8,128)}, u32[]{:S(2)}) copy-start(f32[8,256]{1,0:T(8,128)} %get-tuple-element.12) | copy-start | bytes 24580
  26.5 3.9 %copy-start.1 = (bf16[56,8,8,256]{3,2,1,0:T(8,128)(2,1)S(1)}, bf16[56,8,8,256]{3,2,1,0:T(8,128)(2,1)}, u32[]{:S(2)}) copy-start(bf16[56,8,8,256]{3,2,1,0:T(8,128)(2,1)} %copy.290) | copy-start | bytes 5505028
  36.0 6.0 %copy-start.3 = (bf16[1,2048,448]{1,2,0:T(8,128)(2,1)S(1)}, bf16[1,2048,448]{1,2,0:T(8,128)(2,1)}, u32[]{:S(2)}) copy-start(bf16[1,2048,448]{1,2,0:T(8,128)(2,1)} %param.12) | copy-start | bytes 5505028
  44.9 0.7 copy-start.13
  44.9 2.5 %copy-start.4 = (bf16[1,2048,64]{2,1,0:T(8,128)(2,1)S(1)}, bf16[1,2048,64]{2,1,0:T(8,128)(2,1)}, u32[]{:S(2)}) copy-start(bf16[1,2048,64]{2,1,0:T(8,128)(2,1)} %get-tuple-element.18) | copy-start | bytes 786436
  47.4 0.7 copy-start.16
  53.2 20.0 %all-to-all-start = ((f32[8,1,2048]{2,1,0:T(1,128)}), f32[8,1,2048]{2,1,0:T(1,128)S(1)}, u32[]{:S(2)}, u32[]{:S(2)}) async-start(f32[8,1,2048]{2,1,0:T(1,128)} %stack.5), calls=%async_computation | async-start | bytes 131072 | tf_op jit(solution)/shard_map/all_to_all | solution.py:121
  61.8 124.3 %reduce-scatter.2.cloned.1.call-start = ((), (), s32[]{:S(2)}) async-start(), calls=%async_computation.3 | async-start | bytes 16515072 | tf_op jit(solution)/shard_map/reduce_scatter | solution.py:143
  67.8 5.5 %copy-start.14 = (f32[448]{0:T(512)S(1)}, f32[448]{0:T(512)}, u32[]{:S(2)}) copy-start(f32[448]{0:T(512)} %param.18) | copy-start | bytes 5380
  99.1 0.7 copy-start.9
  99.1 0.8 copy-start.6
  99.2 2.3 copy-start.2
  108.1 6.4 %copy-start.15 = (s32[8]{0:T(128)S(1)}, s32[8]{0:T(128)}, u32[]{:S(2)}) copy-start(s32[8]{0:T(128)} %get-tuple-element.15) | copy-start | bytes 100
  118.2 74.9 %copy-start.12 = (s32[16,8]{0,1:T(8,128)S(1)}, s32[16,8]{0,1:T(8,128)}, u32[]{:S(2)}) copy-start(s32[16,8]{0,1:T(8,128)} %param.21) | copy-start | bytes 1540
  118.2 32.9 %all-to-all-start.1 = ((bf16[16,7,4096]{2,1,0:T(8,128)(2,1)}), bf16[16,7,4096]{2,1,0:T(8,128)(2,1)}, u32[]{:S(2)}, u32[]{:S(2)}) async-start(bf16[16,7,4096]{2,1,0:T(8,128)(2,1)} %copy.260), calls=%async_computation.2 | async-start | bytes 2097152 | tf_op jit(solution)/shard_map/all_to_all | solution.py:152
  188.2 45.4 %collective-permute-start = (bf16[128,3584]{1,0:T(8,128)(2,1)}, bf16[128,3584]{1,0:T(8,128)(2,1)}, u32[]{:S(2)}, u32[]{:S(2)}) collective-permute-start(bf16[128,3584]{1,0:T(8,128)(2,1)} %constant_dynamic-slice_fusion), channel_id=1, source_target_pairs={{0,2},{2,0},{1,3},{3,1},{4,6},{6,4},{5,7},{7,5},{8,10},{10,8},{9,1... | collective-permute-start | bytes 2752520 | tf_op jit(solution)/shard_map/ppermute | solution.py:160
Sparse Core Ops, SparseCore 0:
  99.3 86.7 reduce-scatter.1
